TPU v7x, 32 devices: a whole 2x2x4 slice. The times are simulated.
32 devices in a mesh: group: 2 (over y), seq: 8 (over z, x), chan: 2 (over core).
Axes of the slice: x: 2, y: 2, z: 4, core: 2. Of those that a mesh axis runs over, the one named last changes fastest.
Arguments:
- fresh: bfloat16 [2048, 3, 2048], P(('group', 'seq'), None, 'chan'), parts along dimension 0, may hold values from -6 to 6
- library: bfloat16 [8, 8, 2048], P('seq', None, 'chan'), may hold values from -6 to 6
- block_slot: int32 [8], replicated, may hold values from 0 to 7, each once
- prefix_blocks: int32 [16, 4], P('group'), parts along dimension 0, may hold values from 0 to 7, all different within a row
- short_taps: float32 [3, 3, 2048], P(None, None, 'chan'), may hold values from -4 to 4
- long_filter: float32 [1024, 2048], P('seq', 'chan'), may hold values from -2 to 2
- skip_gain: float32 [2048], P('chan'), may hold values from -6 to 6
Outputs:
- mixed: bfloat16 [2048, 2048], P(('group', 'seq'), 'chan'), parts along dimension 0
There are 2 independent parts, one for each index of `group`. A program takes and returns all parts, laid end to end along the dimension named above; an argument that names none is the same for every part. Nothing has to cross between parts.
Inputs may be any that keep to these rules, and one draw needn't show every extreme that they name: `block_slot`: each number appears once. `prefix_blocks`: every library block is named at least once; the four entries of a row differ.
All inputs are finite; a program needn't handle non-finite values.
Results may differ from a plain program's by a relative error of at most 0.008.
Values may be sent and summed in bfloat16 or wider, within the bound.
No kernel may reach another device: no remote copies, remote signals or barrier semaphores. Data moves between devices by JAX's collectives and lax.ppermute only.
A program may use at most 64 MiB of HBM per device.

v0:
```python
import math
import jax
import jax.numpy as jnp
from jax import lax
from jax.sharding import PartitionSpec as P

TAPS = 3
BLK = 8


def from_behind(shard, axis, by):
    count = lax.axis_size(axis)
    pairs = [(i, i + by) for i in range(count) if 0 <= i + by < count]
    return lax.ppermute(shard, axis, pairs)


def exact_dot(pattern, matrix, tensor):
    return jnp.einsum(pattern, matrix, tensor, precision=lax.Precision.HIGHEST)


def turn_angles(numbers, period):
    return (numbers % period).astype(jnp.float32) * (2.0 * math.pi / period)


def ring_body(fresh, library, block_slot, prefix_blocks, short_taps, long_filter, skip_gain):
    row_count = fresh.shape[0]
    channels = fresh.shape[2]
    devices = lax.axis_size("seq")
    seq_index = lax.axis_index("seq")
    group_rows = row_count // devices
    period = 2 * row_count * devices
    block_ids = jnp.arange(devices, dtype=jnp.int32)
    mode_ids = jnp.arange(2 * devices, dtype=jnp.int32)
    coarse = turn_angles(mode_ids[:, None] * block_ids[None, :], 2 * devices)
    cos_q = jnp.cos(coarse)
    sin_q = jnp.sin(coarse)
    local_rows = seq_index * group_rows + jnp.arange(group_rows, dtype=jnp.int32)
    twist = turn_angles(mode_ids[:, None] * local_rows[None, :], period)
    twist_cos = jnp.cos(twist)[:, :, None]
    twist_sin = jnp.sin(twist)[:, :, None]
    row_ids = jnp.arange(row_count, dtype=jnp.int32)
    fine_angles = turn_angles(row_ids[:, None] * row_ids[None, :], row_count)
    cos_m = jnp.cos(fine_angles)
    sin_m = jnp.sin(fine_angles)
    first_modes = 2 * seq_index + jnp.arange(2, dtype=jnp.int32)
    back_twist = turn_angles(first_modes[:, None] * row_ids[None, :], period)
    back_cos = jnp.cos(back_twist)[:, :, None]
    back_sin = jnp.sin(back_twist)[:, :, None]

    def to_modes(column):
        real_part = exact_dot("kq,qgc->kgc", cos_q, column)
        imag_part = -exact_dot("kq,qgc->kgc", sin_q, column)
        return jnp.stack(
            [
                real_part * twist_cos + imag_part * twist_sin,
                imag_part * twist_cos - real_part * twist_sin,
            ]
        )

    def to_spectrum(spread):
        real_part = exact_dot("ki,jic->jkc", cos_m, spread[0]) + exact_dot(
            "ki,jic->jkc", sin_m, spread[1]
        )
        imag_part = exact_dot("ki,jic->jkc", cos_m, spread[1]) - exact_dot(
            "ki,jic->jkc", sin_m, spread[0]
        )
        return (real_part, imag_part)

    blocks_here = row_count // BLK
    flat_ids = prefix_blocks.reshape(-1)
    first_block = jnp.minimum(seq_index * blocks_here, flat_ids.shape[0] - blocks_here)
    own_ids = lax.dynamic_slice_in_dim(flat_ids, first_block, blocks_here)
    matches = own_ids[:, None] == jnp.arange(block_slot.shape[0], dtype=jnp.int32)[None, :]
    wanted = jnp.sum(jnp.where(matches, block_slot[None, :], 0), axis=1)
    shards = lax.all_gather(library, "seq", axis=0, tiled=True)
    picker = (wanted[:, None] == jnp.arange(shards.shape[0], dtype=jnp.int32)[None, :]).astype(
        jnp.bfloat16
    )
    gathered = jnp.einsum("bn,nlc->blc", picker, shards, preferred_element_type=jnp.float32)
    cached = gathered.reshape(row_count, channels).astype(jnp.bfloat16)
    values = jnp.where(seq_index < devices // 4, cached, fresh[:, 2])
    stacked = jnp.concatenate([fresh[:, :2], values[:, None]], axis=1)
    previous = from_behind(stacked[row_count - (TAPS - 1) :], "seq", 1)
    extended = jnp.concatenate([previous, stacked], axis=0)
    shortened = jnp.zeros((row_count, 3, channels), jnp.float32)
    for offset in range(TAPS):
        window_start = TAPS - 1 - offset
        shortened = shortened + short_taps[offset][None] * extended[
            window_start : window_start + row_count
        ].astype(jnp.float32)
    gating = shortened[:, 0]
    signal = shortened[:, 1] * shortened[:, 2]
    spread_signal = to_modes(
        lax.all_to_all(signal[None], "seq", split_axis=1, concat_axis=0, tiled=True)
    )
    spread_taps = to_modes(
        lax.all_to_all(long_filter[None], "seq", split_axis=1, concat_axis=0, tiled=True)
    )
    moved_signal, moved_taps = (
        lax.all_to_all(
            spread_signal.astype(jnp.bfloat16), "seq", split_axis=1, concat_axis=2, tiled=True
        ).astype(spread_signal.dtype),
        lax.all_to_all(
            spread_taps.astype(jnp.bfloat16), "seq", split_axis=1, concat_axis=2, tiled=True
        ).astype(spread_taps.dtype),
    )
    sig_real, sig_imag = to_spectrum(moved_signal)
    tap_real, tap_imag = to_spectrum(moved_taps)
    prod_real = sig_real * tap_real - sig_imag * tap_imag
    prod_imag = sig_real * tap_imag + sig_imag * tap_real
    back_real = exact_dot("ki,jic->jkc", cos_m, prod_real) - exact_dot(
        "ki,jic->jkc", sin_m, prod_imag
    )
    back_imag = exact_dot("ki,jic->jkc", cos_m, prod_imag) + exact_dot(
        "ki,jic->jkc", sin_m, prod_real
    )
    turned = jnp.stack(
        [back_real * back_cos - back_imag * back_sin, back_imag * back_cos + back_real * back_sin]
    )
    spread = lax.all_to_all(turned, "seq", split_axis=2, concat_axis=1, tiled=True)
    positions = (
        exact_dot("kq,kgc->qgc", cos_q, spread[0]) - exact_dot("kq,kgc->qgc", sin_q, spread[1])
    ) / period
    convolved = lax.all_to_all(positions, "seq", split_axis=0, concat_axis=1, tiled=True)[0]
    output = gating * (convolved + skip_gain[None, :] * signal)
    return output.astype(jnp.bfloat16)


def dft_tables(tokens):
    period = 2 * tokens
    width = 1
    while width * width < tokens:
        width *= 2
    outer = tokens // width
    freqs = jnp.arange(tokens + 1, dtype=jnp.int32)[:, None]
    coarse = turn_angles(freqs * (width * jnp.arange(outer, dtype=jnp.int32))[None, :], period)
    fine = turn_angles(freqs * jnp.arange(width, dtype=jnp.int32)[None, :], period)
    c1, s1 = (jnp.cos(coarse)[:, :, None], jnp.sin(coarse)[:, :, None])
    c2, s2 = (jnp.cos(fine)[:, None, :], jnp.sin(fine)[:, None, :])
    cos_t = (c1 * c2 - s1 * s2).reshape(tokens + 1, tokens)
    sin_t = (s1 * c2 + c1 * s2).reshape(tokens + 1, tokens)
    return (cos_t, sin_t)


def local_body(fresh, library, block_slot, prefix_blocks, short_taps, long_filter, skip_gain):
    row_count, _, channels = fresh.shape
    devices = lax.axis_size("seq")
    seq_index = lax.axis_index("seq")
    tokens = row_count * devices
    own = channels // devices
    lib_here = library.shape[0]
    lib_rows = lib_here * BLK // 4
    packed = jnp.concatenate([fresh, long_filter.astype(jnp.bfloat16)[:, None, :]], axis=1)
    packed = jnp.concatenate([packed, library.reshape(lib_rows, 4, channels)], axis=0)
    packed = packed.reshape(row_count + lib_rows, 4, devices, own).transpose(2, 0, 1, 3)
    moved = lax.all_to_all(packed, "seq", split_axis=0, concat_axis=0, tiled=True)
    rows = moved[:, :row_count].reshape(tokens, 4, own)
    lib_all = moved[:, row_count:].reshape(devices * lib_here, BLK * own)
    slot_ids = block_slot[prefix_blocks.reshape(-1)]
    prefix_len = slot_ids.shape[0] * BLK
    picker = (slot_ids[:, None] == jnp.arange(lib_all.shape[0], dtype=jnp.int32)[None, :]).astype(
        jnp.bfloat16
    )
    cached = jnp.dot(picker, lib_all, preferred_element_type=jnp.float32)
    cached = cached.reshape(prefix_len, own).astype(jnp.bfloat16)
    values = jnp.concatenate([cached, rows[prefix_len:, 2]], axis=0)
    stacked = jnp.concatenate([rows[:, :2], values[:, None]], axis=1).astype(jnp.float32)
    taps = lax.dynamic_slice_in_dim(short_taps, seq_index * own, own, axis=2)
    gain = lax.dynamic_slice_in_dim(skip_gain, seq_index * own, own, axis=0)
    shortened = jnp.zeros((tokens, 3, own), jnp.float32)
    for offset in range(TAPS):
        shifted = jnp.pad(stacked[: tokens - offset], ((offset, 0), (0, 0), (0, 0)))
        shortened = shortened + taps[offset][None] * shifted
    gating = shortened[:, 0]
    signal = shortened[:, 1] * shortened[:, 2]
    cos_t, sin_t = dft_tables(tokens)
    table = jnp.concatenate([cos_t, sin_t], axis=0).astype(jnp.bfloat16)
    operands = jnp.concatenate([signal.astype(jnp.bfloat16), rows[:, 3]], axis=1)
    spec = jnp.dot(table, operands, preferred_element_type=jnp.float32)
    bins = tokens + 1
    sig_c, tap_c = (spec[:bins, :own], spec[:bins, own:])
    sig_s, tap_s = (spec[bins:, :own], spec[bins:, own:])
    weight = jnp.where((jnp.arange(bins) == 0) | (jnp.arange(bins) == tokens), 1.0, 2.0).astype(
        jnp.float32
    )[:, None] / (2 * tokens)
    real = (sig_c * tap_c - sig_s * tap_s) * weight
    turned = (sig_c * tap_s + sig_s * tap_c) * weight
    back = jnp.concatenate([real, turned], axis=0).astype(jnp.bfloat16)
    convolved = lax.dot_general(
        table, back, (((0,), (0,)), ((), ())), preferred_element_type=jnp.float32
    )
    output = (gating * (convolved + gain[None, :] * signal)).astype(jnp.bfloat16)
    output = lax.all_to_all(
        output.reshape(devices, row_count, own), "seq", split_axis=0, concat_axis=0, tiled=True
    )
    return output.transpose(1, 0, 2).reshape(row_count, channels)


def body(fresh, library, *rest):
    devices = lax.axis_size("seq")
    tokens = fresh.shape[0] * devices
    fits = tokens <= 4096 and fresh.shape[2] % devices == 0 and (library.shape[0] * BLK % 4 == 0)
    if fits:
        return local_body(fresh, library, *rest)
    return ring_body(fresh, library, *rest)


def solution(mesh):
    return jax.shard_map(
        body,
        mesh=mesh,
        in_specs=(
            P(("group", "seq"), None, "chan"),
            P("seq", None, "chan"),
            P(),
            P("group", None),
            P(None, None, "chan"),
            P("seq", "chan"),
            P("chan"),
        ),
        out_specs=P(("group", "seq"), "chan"),
        check_vma=False,
    )
```

profile of v0, /device:TPU:0, one launch (start us, length us, event | category | flops | bytes accessed | tf_op | source)
XLA Modules:
  0.0 62.9 jit_solution(6470833181533852721)
XLA Ops:
  0.0 0.0 copy-start
  0.0 0.7 %copy.40 = bf16[1,8,8,128]{3,2,1,0:T(8,128)(2,1)S(1)} copy(bf16[1,8,8,128]{3,1,2,0:T(8,128)(2,1)} %bitcast.60) | data formatting | bytes 32768
  0.7 1.1 %convert_element_type.49 = bf16[128,1024]{1,0:T(8,128)(2,1)S(1)} convert(f32[128,1024]{1,0:T(8,128)} %param.12) | non-fusion elementwise | flops 131072 | bytes 786432 | tf_op jit(solution)/shard_map/convert_element_type | solution.py:153
  1.8 0.2 copy.31
  2.0 2.3 %copy.30 = bf16[128,3,1024]{0,2,1:T(8,128)(2,1)} copy(bf16[128,3,1024]{2,0,1:T(8,128)(2,1)} %param.7) | data formatting | bytes 1572864 | tf_op args[0]
  4.3 0.5 copy.32
  4.8 1.7 %maximum_bitcast_fusion = bf16[8,130,4,128]{1,3,0,2:T(8,128)(2,1)S(1)} fusion(bf16[2,4,8,128]{0,3,2,1:T(8,128)(2,1)S(1)} %copy.32, bf16[128,1,8,128]{0,3,2,1:T(8,128)(2,1)S(1)} %bitcast.56, bf16[128,3,8,128]{0,3,2,1:T(8,128)(2,1)} %bitcast.51), kind=kLoop, calls=%fused_computation.6 | loop fusion | flops 3194880 | bytes 2129920 | tf_op jit(solution)/shard_map/transpose | solution.py:155
  6.5 0.0 copy-start.3
  6.5 2.3 %copy.33 = bf16[8,130,4,128]{3,2,1,0:T(4,128)(2,1)} copy(bf16[8,130,4,128]{1,3,0,2:T(8,128)(2,1)S(1)} %maximum_bitcast_fusion) | data formatting | bytes 2129920 | tf_op jit(solution)/shard_map/transpose | solution.py:155
  8.8 7.3 %all-to-all-start = ((bf16[8,130,4,128]{3,2,1,0:T(4,128)(2,1)}), bf16[8,130,4,128]{3,2,1,0:T(4,128)(2,1)S(1)}, u32[]{:S(2)}, u32[]{:S(2)}) async-start(bf16[8,130,4,128]{3,2,1,0:T(4,128)(2,1)} %copy.33), calls=%async_computation | async-start | bytes 2129920 | tf_op jit(solution)/shard_map/all_to_all | solution.py:156
  16.1 0.0 copy-done.3
  16.1 0.1 copy.35
  16.2 0.1 reshape.176
  16.3 0.8 %dynamic_slice.7 = f32[128]{0:T(128)S(1)} dynamic-slice(f32[1024]{0:T(1024)} %param.13, s32[]{:T(128)S(6)} %select_n.53), dynamic_slice_sizes={128} | dynamic-slice | bytes 1028 | tf_op jit(solution)/shard_map/dynamic_slice | solution.py:169
  17.0 0.0 copy-done
  17.1 0.7 %gather_fusion = s32[32]{0:T(128)S(1)} fusion(s32[8]{0:T(128)S(1)} %copy-done, s32[1024]{0:T(1024)S(1)} %pad_clamp_fusion), kind=kCustom, calls=%fused_computation | custom fusion | bytes 384 | tf_op jit(solution)/shard_map/gather | solution.py:159
  17.8 0.7 %dynamic-slice_bitcast_fusion.2 = (f32[3,128]{1,0:T(4,128)S(1)}, f32[3,128]{1,0:T(4,128)S(1)}, f32[3,128]{1,0:T(4,128)S(1)}) fusion(f32[3,3,1024]{2,1,0:T(4,128)} %param.11, s32[]{:T(128)S(6)} %select_n.53, s32[]{:T(128)S(6)} %add.79, s32[]{:T(128)S(6)} %add.80), kind=kLoop, calls=%fused_computation.61 | loop fusion | bytes 9228 | tf_op jit(solution)/shard_map/mul | solution.py:173
  18.5 0.6 fusion.25
  19.1 0.7 %fusion.28 = (f32[1025,32]{0,1:T(8,128)S(1)}, f32[1025,32]{0,1:T(8,128)S(1)}) fusion(s32[32]{0:T(128)S(1)} %iota_multiply_fusion), kind=kLoop, calls=%fused_computation.50 | loop fusion | flops 459200 | bytes 262528 | tf_op jit(solution)/shard_map/cos | solution.py:138
  19.7 3.7 %subtract_convert_fusion = (bf16[1025,32,32]{0,2,1:T(8,128)(2,1)}, bf16[1025,32,32]{0,2,1:T(8,128)(2,1)}) fusion(f32[1025,32]{0,1:T(8,128)S(1)} %get-tuple-element.14, f32[1025,32]{0,1:T(8,128)S(1)} %get-tuple-element.13, f32[1025,32]{0,1:T(8,128)S(1)} %get-tuple-element.15, f32[1025,32]{0,1:T(8,128)S(1)} %get-tuple-element.12), kind=kLoop, calls=%fused_computation.2 | loop fusion | flops 8396800 | bytes 4723200 | tf_op jit(solution)/shard_map/convert.5
  23.4 18.8 %all-to-all-done = bf16[8,130,4,128]{3,2,1,0:T(4,128)(2,1)S(1)} async-done(((bf16[8,130,4,128]{3,2,1,0:T(4,128)(2,1)}), bf16[8,130,4,128]{3,2,1,0:T(4,128)(2,1)S(1)}, u32[]{:S(2)}, u32[]{:S(2)}) %all-to-all-start) | async-done | bytes 1064992 | tf_op jit(solution)/shard_map/all_to_all | solution.py:156
  42.2 0.4 slice.70
  42.6 0.2 copy.34
  42.9 0.2 convolution_convert_fusion
  43.2 0.1 maximum_convert_fusion
  43.3 0.0 copy-start.1
  43.3 0.0 copy-start.2
  43.4 0.5 multiply_add_fusion
  43.9 0.1 fusion.12
  44.0 1.0 %copy-done.1 = bf16[1025,32,32]{0,2,1:T(8,128)(2,1)S(1)} copy-done((bf16[1025,32,32]{0,2,1:T(8,128)(2,1)S(1)}, bf16[1025,32,32]{0,2,1:T(8,128)(2,1)}, u32[]{:S(2)}) %copy-start.1) | copy-done | bytes 2099224
  45.0 0.7 %copy-done.2 = bf16[1025,32,32]{0,2,1:T(8,128)(2,1)S(1)} copy-done((bf16[1025,32,32]{0,2,1:T(8,128)(2,1)S(1)}, bf16[1025,32,32]{0,2,1:T(8,128)(2,1)}, u32[]{:S(2)}) %copy-start.2) | copy-done | bytes 2099224
  45.7 2.2 %fusion.1 = f32[2050,256]{1,0:T(8,128)S(1)} fusion(bf16[1025,1024]{0,1:T(8,128)(2,1)S(1)} %bitcast.54, bf16[1025,1024]{0,1:T(8,128)(2,1)S(1)} %bitcast.52, bf16[1024,128]{1,0:T(8,128)(2,1)S(1)} %slice_bitcast_fusion.1, bf16[1024,128]{1,0:T(8,128)(2,1)S(1)} %fusion.12), kind=kOutput, calls=%fused_computation.5 | convolution fusion | flops 1084235776 | bytes 6821888 | tf_op jit(solution)/shard_map/dot_general | solution.py:179
  47.9 0.3 multiply_convert_fusion.1
  48.2 1.4 %fusion.4 = bf16[1024,128]{1,0:T(8,128)(2,1)S(1)} fusion(bf16[1025,1024]{0,1:T(8,128)(2,1)S(1)} %bitcast.55, bf16[1025,1024]{0,1:T(8,128)(2,1)S(1)} %bitcast.53, bf16[1025,128]{1,0:T(8,128)(2,1)S(1)} %get-tuple-element.6, bf16[1025,128]{1,0:T(8,128)(2,1)S(1)} %get-tuple-element.5, f32[1024,3,128]{2,0,1:T(8,128)S(1)} %multiply_add_fusion, ...), kind=kOutput, calls=%fused_computation.10 | convolution fusion | flops 547496960 | bytes 6558720 | tf_op jit(solution)/shard_map/dot_general | solution.py:189
  49.6 12.5 %all_to_all.10 = bf16[8,128,128]{2,1,0:T(8,128)(2,1)S(1)} all-to-all(bf16[8,128,128]{2,1,0:T(8,128)(2,1)S(1)} %bitcast.57), channel_id=1, replica_groups=mesh['group'=2,'seq'=8,'chan'=2] {'seq'}, dimensions={0} | all-to-all | bytes 524288 | tf_op jit(solution)/shard_map/all_to_all | solution.py:193
  62.1 0.7 %copy_bitcast_fusion = bf16[128,1024]{1,0:T(8,128)(2,1)} fusion(bf16[8,128,128]{2,1,0:T(8,128)(2,1)S(1)} %all_to_all.10), kind=kLoop, calls=%fused_computation.24 | loop fusion | bytes 524288 | tf_op jit(solution)/shard_map/reshape | solution.py:196
  (11 shorter events, 0.2 us)
Async XLA Ops:
  0.0 17.0 %copy-start = (s32[8]{0:T(128)S(1)}, s32[8]{0:T(128)}, u32[]{:S(2)}) copy-start(s32[8]{0:T(128)} %param.9) | copy-start | bytes 100
  6.5 9.6 %copy-start.3 = (s32[8,4]{0,1:T(4,128)S(1)}, s32[8,4]{0,1:T(4,128)}, u32[]{:S(2)}) copy-start(s32[8,4]{0,1:T(4,128)} %param.10) | copy-start | bytes 388
  8.8 33.4 %all-to-all-start = ((bf16[8,130,4,128]{3,2,1,0:T(4,128)(2,1)}), bf16[8,130,4,128]{3,2,1,0:T(4,128)(2,1)S(1)}, u32[]{:S(2)}, u32[]{:S(2)}) async-start(bf16[8,130,4,128]{3,2,1,0:T(4,128)(2,1)} %copy.33), calls=%async_computation | async-start | bytes 2129920 | tf_op jit(solution)/shard_map/all_to_all | solution.py:156
  43.3 1.7 %copy-start.1 = (bf16[1025,32,32]{0,2,1:T(8,128)(2,1)S(1)}, bf16[1025,32,32]{0,2,1:T(8,128)(2,1)}, u32[]{:S(2)}) copy-start(bf16[1025,32,32]{0,2,1:T(8,128)(2,1)} %get-tuple-element.7) | copy-start | bytes 6297604
  43.3 2.4 %copy-start.2 = (bf16[1025,32,32]{0,2,1:T(8,128)(2,1)S(1)}, bf16[1025,32,32]{0,2,1:T(8,128)(2,1)}, u32[]{:S(2)}) copy-start(bf16[1025,32,32]{0,2,1:T(8,128)(2,1)} %get-tuple-element.8) | copy-start | bytes 6297604
where the time goes:
time: 63.3 us; the launch traced here: 62.9 us
  waiting for transfers between devices  18.8 us (30%)
  blocking collectives  12.5 us (20%)
  local copies, waits for them, and re-layouts  11.6 us (18%)
  other arithmetic  8.75 us (14%)
  starting transfers between devices  7.28 us (12%)
  matrix products  3.8 us (6%)
    all_to_all x1, waiting for transfers between devices, local_body(): lax.all_to_all(packed, 'seq', split_axis=0, concat_axis=0, tiled=True)  18.8 us
    all_to_all x1, blocking collectives, local_body(): lax.all_to_all(output.reshape(devices, row_count, own), 'seq', split_axis...  12.5 us
    all_to_all x1, starting transfers between devices, local_body(): lax.all_to_all(packed, 'seq', split_axis=0, concat_axis=0, tiled=True)  7.28 us
    unnamed x12, local copies, waits for them, and re-layouts  4.87 us
    another operation x2, other arithmetic  3.99 us
    transpose x1, local copies, waits for them, and re-layouts, local_body(): packed.reshape(row_count + lib_rows, 4, devices, own).transpose(2, 0, 1, 3)  2.29 us
    dot_general x1, matrix products, local_body(): spec = jnp.dot(table, operands, preferred_element_type=jnp.float32)  2.2 us
    transpose x1, other arithmetic, local_body(): packed.reshape(row_count + lib_rows, 4, devices, own).transpose(2, 0, 1, 3)  1.7 us
  transfers between devices with their start and end apart: 1, of which 1 were waited for; matrix products, arithmetic and copies ran while one was open for 12% of the time, Pallas kernels for 0%

commit v1 on v0

--- a/solution.py
+++ b/solution.py
@@ -6,6 +6,22 @@
 
 TAPS = 3
 BLK = 8
+
+
+def swapped_with_each(array, axis, split, join):
+    ways, here = (lax.axis_size(axis), lax.axis_index(axis))
+    width = array.shape[split] // ways
+    dims = list(array.shape)
+    dims[split] = width
+    height = dims[join]
+    dims[join] = height * ways
+    full = jnp.zeros(dims, array.dtype)
+    for mask in range(ways):
+        part = lax.dynamic_slice_in_dim(array, (here ^ mask) * width, width, axis=split)
+        if mask:
+            part = lax.ppermute(part, axis, [(d, d ^ mask) for d in range(ways)])
+        full = lax.dynamic_update_slice_in_dim(full, part, (here ^ mask) * height, axis=join)
+    return full
 
 
 def from_behind(shard, axis, by):
@@ -153,7 +169,7 @@
     packed = jnp.concatenate([fresh, long_filter.astype(jnp.bfloat16)[:, None, :]], axis=1)
     packed = jnp.concatenate([packed, library.reshape(lib_rows, 4, channels)], axis=0)
     packed = packed.reshape(row_count + lib_rows, 4, devices, own).transpose(2, 0, 1, 3)
-    moved = lax.all_to_all(packed, "seq", split_axis=0, concat_axis=0, tiled=True)
+    moved = swapped_with_each(packed, "seq", 0, 0)
     rows = moved[:, :row_count].reshape(tokens, 4, own)
     lib_all = moved[:, row_count:].reshape(devices * lib_here, BLK * own)
     slot_ids = block_slot[prefix_blocks.reshape(-1)]

time: 63.3 us -> 101 us (1.60)
  local copies, waits for them, and re-layouts: 11.6 us -> 61.2 us
  waiting for transfers between devices: 18.8 us -> 0.33 us
  starting transfers between devices: 7.28 us -> 14.6 us
  other arithmetic: 8.75 us -> 7.08 us
    dynamic_update_slice x0 -> x8, local copies, waits for them, and re-layouts: none -> 51 us  [swapped_with_each(): lax.dynamic_update_slice_in_dim(full, part, (here ^ mask) * height, axis=...]
    all_to_all x1 -> x0, waiting for transfers between devices: 18.8 us -> none  [local_body(): lax.all_to_all(packed, 'seq', split_axis=0, concat_axis=0, tiled=True)]
    ppermute x0 -> x7, starting transfers between devices: none -> 14.6 us  [swapped_with_each(): part = lax.ppermute(part, axis, [(d, d ^ mask) for d in range(ways)])]
    all_to_all x1 -> x0, starting transfers between devices: 7.28 us -> none  [local_body(): lax.all_to_all(packed, 'seq', split_axis=0, concat_axis=0, tiled=True)]
    ppermute x0 -> x7, local copies, waits for them, and re-layouts: none -> 3.26 us  [swapped_with_each(): part = lax.ppermute(part, axis, [(d, d ^ mask) for d in range(ways)])]
    transpose x1 -> x0, local copies, waits for them, and re-layouts: 2.29 us -> none  [local_body(): packed.reshape(row_count + lib_rows, 4, devices, own).transpose(2, 0, 1, 3)]
    unnamed x12 -> x13, local copies, waits for them, and re-layouts: 4.87 us -> 2.69 us
    transpose x1 -> x0, other arithmetic: 1.7 us -> none  [local_body(): packed.reshape(row_count + lib_rows, 4, devices, own).transpose(2, 0, 1, 3)]
  transfers between devices with their start and end apart: 1 -> 7, of which waited for: 1 -> 1; matrix products, arithmetic and copies ran while one was open for 12% -> 55% of each run, Pallas kernels for 0% -> 0%
where the time goes in v1:
time: 101 us; the launch traced here: 100 us
  local copies, waits for them, and re-layouts  61.2 us (61%)
  starting transfers between devices  14.6 us (14%)
  blocking collectives  12.9 us (13%)
  other arithmetic  7.08 us (7%)
  matrix products  3.79 us (4%)
    dynamic_update_slice x8, local copies, waits for them, and re-layouts, swapped_with_each(): lax.dynamic_update_slice_in_dim(full, part, (here ^ mask) * height, axis=...  51 us
    ppermute x7, starting transfers between devices, swapped_with_each(): part = lax.ppermute(part, axis, [(d, d ^ mask) for d in range(ways)])  14.6 us
    all_to_all x1, blocking collectives, local_body(): lax.all_to_all(output.reshape(devices, row_count, own), 'seq', split_axis...  12.9 us
    another operation x2, other arithmetic  3.93 us
    ppermute x7, local copies, waits for them, and re-layouts, swapped_with_each(): part = lax.ppermute(part, axis, [(d, d ^ mask) for d in range(ways)])  3.26 us
    unnamed x13, local copies, waits for them, and re-layouts  2.69 us
    dot_general x1, matrix products, local_body(): spec = jnp.dot(table, operands, preferred_element_type=jnp.float32)  2.19 us
  transfers between devices with their start and end apart: 7, of which 1 were waited for; matrix products, arithmetic and copies ran while one was open for 55% of the time, Pallas kernels for 0%

profile of v1, /device:TPU:0, one launch (start us, length us, event | category | flops | bytes accessed | tf_op | source)
XLA Modules:
  0.0 100.4 jit_solution(4167126773007965421)
XLA Ops:
  0.0 0.0 copy-start
  0.0 0.8 copy.28
  0.8 1.1 %convert_bitcast_fusion = bf16[16,8,8,128]{3,1,2,0:T(8,128)(2,1)S(1)} fusion(f32[128,1024]{1,0:T(8,128)} %param.12), kind=kLoop, calls=%fused_computation.28 | loop fusion | flops 131072 | bytes 786432
  2.0 0.0 copy-done
  2.0 0.2 copy_bitcast_fusion
  2.3 0.0 copy-start.4
  2.3 0.1 pad_maximum_fusion.9
  2.4 0.1 dynamic-slice_bitcast_fusion
  2.5 6.1 %collective-permute-start.6 = (bf16[1,130,4,128]{3,1,2,0:T(8,128)(2,1)S(1)}, bf16[1,130,4,128]{3,1,2,0:T(8,128)(2,1)S(1)}, u32[]{:S(2)}, u32[]{:S(2)}) collective-permute-start(bf16[1,130,4,128]{3,1,2,0:T(8,128)(2,1)S(1)} %get-tuple-element.7), channel_id=1, source_target_pairs={{0,14},{2,12},{4,10},{6,8},{8,6},{10,4},{12,2},{14,0},{1,15},{3,13... | collective-permute-start | bytes 399368 | tf_op jit(solution)/shard_map/ppermute | solution.py:22
  8.6 0.2 collective-permute-start.5
  8.8 0.8 collective-permute-start.4
  9.5 3.4 %collective-permute-start.1 = (bf16[1,130,4,128]{3,1,2,0:T(8,128)(2,1)S(1)}, bf16[1,130,4,128]{3,1,2,0:T(8,128)(2,1)S(1)}, u32[]{:S(2)}, u32[]{:S(2)}) collective-permute-start(bf16[1,130,4,128]{3,1,2,0:T(8,128)(2,1)S(1)} %get-tuple-element.12), channel_id=1, source_target_pairs={{0,4},{2,6},{4,0},{6,2},{8,12},{10,14},{12,8},{14,10},{1,5},{3,7},... | collective-permute-start | bytes 399368 | tf_op jit(solution)/shard_map/ppermute | solution.py:22
  12.9 1.5 %collective-permute-start = (bf16[1,130,4,128]{3,1,2,0:T(8,128)(2,1)S(1)}, bf16[1,130,4,128]{3,1,2,0:T(8,128)(2,1)S(1)}, u32[]{:S(2)}, u32[]{:S(2)}) collective-permute-start(bf16[1,130,4,128]{3,1,2,0:T(8,128)(2,1)S(1)} %get-tuple-element.13), channel_id=1, source_target_pairs={{0,2},{2,0},{4,6},{6,4},{8,10},{10,8},{12,14},{14,12},{1,3},{3,1},... | collective-permute-start | bytes 399368 | tf_op jit(solution)/shard_map/ppermute | solution.py:22
  14.4 0.6 fusion.25
  15.0 0.0 copy-done.4
  15.0 0.1 copy.23
  15.1 0.1 reshape.184
  15.2 0.7 fusion.28
  15.8 0.0 copy-start.1
  15.8 3.6 %subtract_convert_fusion = (bf16[1025,32,32]{0,2,1:T(8,128)(2,1)}, bf16[1025,32,32]{0,2,1:T(8,128)(2,1)}) fusion(f32[1025,32]{0,1:T(8,128)S(1)} %get-tuple-element.22, f32[1025,32]{0,1:T(8,128)S(1)} %get-tuple-element.21, f32[1025,32]{0,1:T(8,128)S(1)} %get-tuple-element.23, f32[1025,32]{0,1:T(8,128)S(1)} %get-tuple-element.20), kind=kLoop, calls=%fused_computation.2 | loop fusion | flops 8396800 | bytes 4723200 | tf_op jit(solution)/shard_map/convert.5
  19.5 0.7 fusion.32
  20.2 0.3 collective-permute-done.1
  20.5 1.5 %collective-permute-start.3 = (bf16[1,130,4,128]{3,1,2,0:T(8,128)(2,1)S(1)}, bf16[1,130,4,128]{3,1,2,0:T(8,128)(2,1)}, u32[]{:S(2)}, u32[]{:S(2)}) collective-permute-start(bf16[1,130,4,128]{3,1,2,0:T(8,128)(2,1)S(1)} %get-tuple-element.10), channel_id=1, source_target_pairs={{0,8},{2,10},{4,12},{6,14},{8,0},{10,2},{12,4},{14,6},{1,9},{3,11}... | collective-permute-start | bytes 399368 | tf_op jit(solution)/shard_map/ppermute | solution.py:22
  22.0 0.0 collective-permute-done
  22.0 1.2 %collective-permute-start.2 = (bf16[1,130,4,128]{3,1,2,0:T(8,128)(2,1)S(1)}, bf16[1,130,4,128]{3,1,2,0:T(8,128)(2,1)}, u32[]{:S(2)}, u32[]{:S(2)}) collective-permute-start(bf16[1,130,4,128]{3,1,2,0:T(8,128)(2,1)S(1)} %get-tuple-element.11), channel_id=1, source_target_pairs={{0,6},{2,4},{4,2},{6,0},{8,14},{10,12},{12,10},{14,8},{1,7},{3,5},... | collective-permute-start | bytes 399368 | tf_op jit(solution)/shard_map/ppermute | solution.py:22
  23.3 0.8 dynamic_slice.39
  24.0 0.2 copy.14
  24.2 0.0 copy-done.1
  24.2 0.7 gather_fusion
  24.9 0.1 broadcast_in_dim.10
  25.1 6.5 %dynamic_update_slice.24 = bf16[8,130,4,128]{3,0,2,1:T(8,128)(2,1)S(1)} dynamic-update-slice(bf16[8,130,4,128]{3,0,2,1:T(8,128)(2,1)S(1)} %broadcast_in_dim.10, bf16[1,130,4,128]{3,0,2,1:T(2,128)(2,1)S(1)} %copy.14, s32[]{:T(128)S(6)} %select_n.86, s32[]{:T(128)} %constant.22.clone.1, s32[]{:T(128)} %constant.22.clone.1, s32[]{:T(128)} %constant.22.clone.1) | dynamic-update-slice | bytes 266244 | tf_op jit(solution)/shard_map/dynamic_update_slice | solution.py:23
  31.6 0.2 copy.15
  31.9 6.4 %dynamic_update_slice.25 = bf16[8,130,4,128]{3,0,2,1:T(8,128)(2,1)S(1)} dynamic-update-slice(bf16[8,130,4,128]{3,0,2,1:T(8,128)(2,1)S(1)} %dynamic_update_slice.24, bf16[1,130,4,128]{3,0,2,1:T(2,128)(2,1)S(1)} %copy.15, s32[]{:T(128)S(6)} %select_n.87, s32[]{:T(128)} %constant.22.clone.1, s32[]{:T(128)} %constant.22.clone.1, s32[]{:T(128)} %constant.22.clone.1) | dynamic-update-slice | bytes 266244 | tf_op jit(solution)/shard_map/dynamic_update_slice | solution.py:23
  38.2 0.2 copy.16
  38.4 6.4 %dynamic_update_slice.26 = bf16[8,130,4,128]{3,0,2,1:T(8,128)(2,1)S(1)} dynamic-update-slice(bf16[8,130,4,128]{3,0,2,1:T(8,128)(2,1)S(1)} %dynamic_update_slice.25, bf16[1,130,4,128]{3,0,2,1:T(2,128)(2,1)S(1)} %copy.16, s32[]{:T(128)S(6)} %select_n.88, s32[]{:T(128)} %constant.22.clone.1, s32[]{:T(128)} %constant.22.clone.1, s32[]{:T(128)} %constant.22.clone.1) | dynamic-update-slice | bytes 266244 | tf_op jit(solution)/shard_map/dynamic_update_slice | solution.py:23
  44.8 0.0 collective-permute-done.2
  44.8 1.1 %copy.17 = bf16[1,130,4,128]{3,0,2,1:T(2,128)(2,1)S(1)} copy(bf16[1,130,4,128]{3,1,2,0:T(8,128)(2,1)} %collective-permute-done.2) | data formatting | bytes 266240 | tf_op jit(solution)/shard_map/ppermute | solution.py:22
  45.9 6.4 %dynamic_update_slice.27 = bf16[8,130,4,128]{3,0,2,1:T(8,128)(2,1)S(1)} dynamic-update-slice(bf16[8,130,4,128]{3,0,2,1:T(8,128)(2,1)S(1)} %dynamic_update_slice.26, bf16[1,130,4,128]{3,0,2,1:T(2,128)(2,1)S(1)} %copy.17, s32[]{:T(128)S(6)} %select_n.89, s32[]{:T(128)} %constant.22.clone.1, s32[]{:T(128)} %constant.22.clone.1, s32[]{:T(128)} %constant.22.clone.1) | dynamic-update-slice | bytes 266244 | tf_op jit(solution)/shard_map/dynamic_update_slice | solution.py:23
  52.3 0.0 collective-permute-done.3
  52.3 1.1 %copy.18 = bf16[1,130,4,128]{3,0,2,1:T(2,128)(2,1)S(1)} copy(bf16[1,130,4,128]{3,1,2,0:T(8,128)(2,1)} %collective-permute-done.3) | data formatting | bytes 266240 | tf_op jit(solution)/shard_map/ppermute | solution.py:22
  53.4 6.4 %dynamic_update_slice.28 = bf16[8,130,4,128]{3,0,2,1:T(8,128)(2,1)S(1)} dynamic-update-slice(bf16[8,130,4,128]{3,0,2,1:T(8,128)(2,1)S(1)} %dynamic_update_slice.27, bf16[1,130,4,128]{3,0,2,1:T(2,128)(2,1)S(1)} %copy.18, s32[]{:T(128)S(6)} %select_n.90, s32[]{:T(128)} %constant.22.clone.1, s32[]{:T(128)} %constant.22.clone.1, s32[]{:T(128)} %constant.22.clone.1) | dynamic-update-slice | bytes 266244 | tf_op jit(solution)/shard_map/dynamic_update_slice | solution.py:23
  59.8 0.0 collective-permute-done.4
  59.8 0.2 copy.19
  60.0 6.4 %dynamic_update_slice.29 = bf16[8,130,4,128]{3,0,2,1:T(8,128)(2,1)S(1)} dynamic-update-slice(bf16[8,130,4,128]{3,0,2,1:T(8,128)(2,1)S(1)} %dynamic_update_slice.28, bf16[1,130,4,128]{3,0,2,1:T(2,128)(2,1)S(1)} %copy.19, s32[]{:T(128)S(6)} %select_n.91, s32[]{:T(128)} %constant.22.clone.1, s32[]{:T(128)} %constant.22.clone.1, s32[]{:T(128)} %constant.22.clone.1) | dynamic-update-slice | bytes 266244 | tf_op jit(solution)/shard_map/dynamic_update_slice | solution.py:23
  66.4 0.0 collective-permute-done.5
  66.4 0.2 copy.20
  66.6 6.4 %dynamic_update_slice.30 = bf16[8,130,4,128]{3,0,2,1:T(8,128)(2,1)S(1)} dynamic-update-slice(bf16[8,130,4,128]{3,0,2,1:T(8,128)(2,1)S(1)} %dynamic_update_slice.29, bf16[1,130,4,128]{3,0,2,1:T(2,128)(2,1)S(1)} %copy.20, s32[]{:T(128)S(6)} %select_n.92, s32[]{:T(128)} %constant.22.clone.1, s32[]{:T(128)} %constant.22.clone.1, s32[]{:T(128)} %constant.22.clone.1) | dynamic-update-slice | bytes 266244 | tf_op jit(solution)/shard_map/dynamic_update_slice | solution.py:23
  72.9 0.0 collective-permute-done.6
  73.0 0.2 copy.21
  73.2 6.4 %dynamic_update_slice.31 = bf16[8,130,4,128]{3,0,2,1:T(8,128)(2,1)S(1)} dynamic-update-slice(bf16[8,130,4,128]{3,0,2,1:T(8,128)(2,1)S(1)} %dynamic_update_slice.30, bf16[1,130,4,128]{3,0,2,1:T(2,128)(2,1)S(1)} %copy.21, s32[]{:T(128)S(6)} %select_n.93, s32[]{:T(128)} %constant.22.clone.1, s32[]{:T(128)} %constant.22.clone.1, s32[]{:T(128)} %constant.22.clone.1) | dynamic-update-slice | bytes 266244 | tf_op jit(solution)/shard_map/dynamic_update_slice | solution.py:23
  79.5 0.1 slice.70
  79.6 0.4 copy.22
  80.1 0.2 convolution_convert_fusion
  80.4 0.1 maximum_convert_fusion
  80.5 0.0 copy-start.2
  80.5 0.5 multiply_add_fusion
  81.1 0.1 fusion.12
  81.1 1.0 %copy-done.2 = bf16[1025,32,32]{0,2,1:T(8,128)(2,1)S(1)} copy-done((bf16[1025,32,32]{0,2,1:T(8,128)(2,1)S(1)}, bf16[1025,32,32]{0,2,1:T(8,128)(2,1)}, u32[]{:S(2)}) %copy-start.2) | copy-done | bytes 2099224
  82.2 0.7 copy-done.3
  82.9 2.2 %fusion.1 = f32[2050,256]{1,0:T(8,128)S(1)} fusion(bf16[1025,1024]{0,1:T(8,128)(2,1)S(1)} %bitcast.75, bf16[1025,1024]{0,1:T(8,128)(2,1)S(1)} %bitcast.73, bf16[1024,128]{1,0:T(8,128)(2,1)S(1)} %slice_bitcast_fusion.1, bf16[1024,128]{1,0:T(8,128)(2,1)S(1)} %fusion.12), kind=kOutput, calls=%fused_computation.5 | convolution fusion | flops 1084235776 | bytes 6821888 | tf_op jit(solution)/shard_map/dot_general | solution.py:195
  85.1 0.3 multiply_convert_fusion.1
  85.4 1.4 %fusion.4 = bf16[1024,128]{1,0:T(8,128)(2,1)S(1)} fusion(bf16[1025,1024]{0,1:T(8,128)(2,1)S(1)} %bitcast.76, bf16[1025,1024]{0,1:T(8,128)(2,1)S(1)} %bitcast.74, bf16[1025,128]{1,0:T(8,128)(2,1)S(1)} %get-tuple-element.6, bf16[1025,128]{1,0:T(8,128)(2,1)S(1)} %get-tuple-element.5, f32[1024,3,128]{2,0,1:T(8,128)S(1)} %multiply_add_fusion, ...), kind=kOutput, calls=%fused_computation.9 | convolution fusion | flops 547496960 | bytes 6558720 | tf_op jit(solution)/shard_map/dot_general | solution.py:205
  86.8 12.9 %all_to_all.5 = bf16[8,128,128]{2,1,0:T(8,128)(2,1)S(1)} all-to-all(bf16[8,128,128]{2,1,0:T(8,128)(2,1)S(1)} %bitcast.78), channel_id=1, replica_groups=mesh['group'=2,'seq'=8,'chan'=2] {'seq'}, dimensions={0} | all-to-all | bytes 524288 | tf_op jit(solution)/shard_map/all_to_all | solution.py:209
  99.6 0.7 copy_bitcast_fusion.1
  (14 shorter events, 0.2 us)
Async XLA Ops:
  0.0 2.0 %copy-start = (bf16[128,3,1024]{2,0,1:T(8,128)(2,1)S(1)}, bf16[128,3,1024]{2,0,1:T(8,128)(2,1)}, u32[]{:S(2)}) copy-start(bf16[128,3,1024]{2,0,1:T(8,128)(2,1)} %param.7) | copy-start | bytes 2359300
  2.3 12.7 %copy-start.4 = (s32[8,4]{0,1:T(4,128)S(1)}, s32[8,4]{0,1:T(4,128)}, u32[]{:S(2)}) copy-start(s32[8,4]{0,1:T(4,128)} %param.10) | copy-start | bytes 388
  2.5 70.5 %collective-permute-start.6 = (bf16[1,130,4,128]{3,1,2,0:T(8,128)(2,1)S(1)}, bf16[1,130,4,128]{3,1,2,0:T(8,128)(2,1)S(1)}, u32[]{:S(2)}, u32[]{:S(2)}) collective-permute-start(bf16[1,130,4,128]{3,1,2,0:T(8,128)(2,1)S(1)} %get-tuple-element.7), channel_id=1, source_target_pairs={{0,14},{2,12},{4,10},{6,8},{8,6},{10,4},{12,2},{14,0},{1,15},{3,13... | collective-permute-start | bytes 399368 | tf_op jit(solution)/shard_map/ppermute | solution.py:22
  8.6 57.8 %collective-permute-start.5 = (bf16[1,130,4,128]{3,1,2,0:T(8,128)(2,1)S(1)}, bf16[1,130,4,128]{3,1,2,0:T(8,128)(2,1)S(1)}, u32[]{:S(2)}, u32[]{:S(2)}) collective-permute-start(bf16[1,130,4,128]{3,1,2,0:T(8,128)(2,1)S(1)} %get-tuple-element.8), channel_id=1, source_target_pairs={{0,12},{2,14},{4,8},{6,10},{8,4},{10,6},{12,0},{14,2},{1,13},{3,15... | collective-permute-start | bytes 399368 | tf_op jit(solution)/shard_map/ppermute | solution.py:22
  8.8 51.0 %collective-permute-start.4 = (bf16[1,130,4,128]{3,1,2,0:T(8,128)(2,1)S(1)}, bf16[1,130,4,128]{3,1,2,0:T(8,128)(2,1)S(1)}, u32[]{:S(2)}, u32[]{:S(2)}) collective-permute-start(bf16[1,130,4,128]{3,1,2,0:T(8,128)(2,1)S(1)} %get-tuple-element.9), channel_id=1, source_target_pairs={{0,10},{2,8},{4,14},{6,12},{8,2},{10,0},{12,6},{14,4},{1,11},{3,9}... | collective-permute-start | bytes 399368 | tf_op jit(solution)/shard_map/ppermute | solution.py:22
  9.5 11.0 %collective-permute-start.1 = (bf16[1,130,4,128]{3,1,2,0:T(8,128)(2,1)S(1)}, bf16[1,130,4,128]{3,1,2,0:T(8,128)(2,1)S(1)}, u32[]{:S(2)}, u32[]{:S(2)}) collective-permute-start(bf16[1,130,4,128]{3,1,2,0:T(8,128)(2,1)S(1)} %get-tuple-element.12), channel_id=1, source_target_pairs={{0,4},{2,6},{4,0},{6,2},{8,12},{10,14},{12,8},{14,10},{1,5},{3,7},... | collective-permute-start | bytes 399368 | tf_op jit(solution)/shard_map/ppermute | solution.py:22
  12.9 9.1 %collective-permute-start = (bf16[1,130,4,128]{3,1,2,0:T(8,128)(2,1)S(1)}, bf16[1,130,4,128]{3,1,2,0:T(8,128)(2,1)S(1)}, u32[]{:S(2)}, u32[]{:S(2)}) collective-permute-start(bf16[1,130,4,128]{3,1,2,0:T(8,128)(2,1)S(1)} %get-tuple-element.13), channel_id=1, source_target_pairs={{0,2},{2,0},{4,6},{6,4},{8,10},{10,8},{12,14},{14,12},{1,3},{3,1},... | collective-permute-start | bytes 399368 | tf_op jit(solution)/shard_map/ppermute | solution.py:22
  15.8 8.4 %copy-start.1 = (s32[8]{0:T(128)S(1)}, s32[8]{0:T(128)}, u32[]{:S(2)}) copy-start(s32[8]{0:T(128)} %param.9) | copy-start | bytes 100
  20.5 31.8 %collective-permute-start.3 = (bf16[1,130,4,128]{3,1,2,0:T(8,128)(2,1)S(1)}, bf16[1,130,4,128]{3,1,2,0:T(8,128)(2,1)}, u32[]{:S(2)}, u32[]{:S(2)}) collective-permute-start(bf16[1,130,4,128]{3,1,2,0:T(8,128)(2,1)S(1)} %get-tuple-element.10), channel_id=1, source_target_pairs={{0,8},{2,10},{4,12},{6,14},{8,0},{10,2},{12,4},{14,6},{1,9},{3,11}... | collective-permute-start | bytes 399368 | tf_op jit(solution)/shard_map/ppermute | solution.py:22
  22.0 22.8 %collective-permute-start.2 = (bf16[1,130,4,128]{3,1,2,0:T(8,128)(2,1)S(1)}, bf16[1,130,4,128]{3,1,2,0:T(8,128)(2,1)}, u32[]{:S(2)}, u32[]{:S(2)}) collective-permute-start(bf16[1,130,4,128]{3,1,2,0:T(8,128)(2,1)S(1)} %get-tuple-element.11), channel_id=1, source_target_pairs={{0,6},{2,4},{4,2},{6,0},{8,14},{10,12},{12,10},{14,8},{1,7},{3,5},... | collective-permute-start | bytes 399368 | tf_op jit(solution)/shard_map/ppermute | solution.py:22
  80.5 1.7 %copy-start.2 = (bf16[1025,32,32]{0,2,1:T(8,128)(2,1)S(1)}, bf16[1025,32,32]{0,2,1:T(8,128)(2,1)}, u32[]{:S(2)}) copy-start(bf16[1025,32,32]{0,2,1:T(8,128)(2,1)} %get-tuple-element.15) | copy-start | bytes 6297604
  80.5 2.4 %copy-start.3 = (bf16[1025,32,32]{0,2,1:T(8,128)(2,1)S(1)}, bf16[1025,32,32]{0,2,1:T(8,128)(2,1)}, u32[]{:S(2)}) copy-start(bf16[1025,32,32]{0,2,1:T(8,128)(2,1)} %get-tuple-element.16) | copy-start | bytes 6297604
